TPU v7x, 32 devices: a whole 2x2x4 slice. The times are simulated.
32 devices in a mesh: group: 2 (over x), dev: 16 (over z, y, core).
Axes of the slice: x: 2, y: 2, z: 4, core: 2. Of those that a mesh axis runs over, the one named last changes fastest.
Arguments:
- suffix_x: bfloat16 [2, 4096, 1600], P('group', 'dev'), may hold values from -6 to 6
- suffix_query: bfloat16 [2, 4096, 1024], P('group', 'dev'), may hold values from -128 to 128
- suffix_keyval: bfloat16 [2, 4096, 2048], P('group', 'dev'), may hold values from -6 to 6
- prefix_keyval: bfloat16 [2, 128, 2048], P('group', 'dev'), may hold values from -6 to 6
- prefix_hidden: bfloat16 [2, 128, 1600], P('group', 'dev'), may hold values from -6 to 6
- kv_weight: bfloat16 [1600, 2048], replicated, may hold values from -0.15625 to 0.15625
- out_weight: bfloat16 [1024, 1600], replicated, may hold values from -0.1875 to 0.1875
- fc_weight: bfloat16 [1600, 3840], P(None, ('group', 'dev')), may hold values from -0.15625 to 0.15625
- proj_weight: bfloat16 [3840, 1600], P(('group', 'dev')), may hold values from -0.09375 to 0.09375
- lengths: int32 [2, 16], P('group'), may hold values from 1 to 256, 2048 in all within a row
- placement: int32 [2, 16], P('group'), may hold values from 0 to 15, each once within a row
- owners: int32 [2, 16], P('group'), may hold values from 0 to 15, each once within a row
- recompute: int32 [2, 2], P('group'), may hold values from 0 to 15
Outputs:
- layer_out: bfloat16 [2, 4096, 1600], P('group', 'dev')
All inputs are finite; a program needn't handle non-finite values.
Results may differ from a plain program's by a relative error of at most 0.008.
Values may be sent and summed in bfloat16 or wider, within the bound.
No kernel may reach another device: no remote copies, remote signals or barrier semaphores. Data moves between devices by JAX's collectives and lax.ppermute only.
A program may use at most 128 MiB of HBM per device.

v0:
```python
import jax
import jax.numpy as jnp
from jax import lax
from jax.sharding import PartitionSpec as P

HEAD_DIM = 64
NEGATIVE = -1e30
EPSILON = 1e-05
SCORE_SCALE = 0.125


def normalize(values_in):
    values_in = values_in.astype(jnp.float32)
    average = jnp.mean(values_in, axis=-1, keepdims=True)
    centered = values_in - average
    variance = jnp.mean(centered * centered, axis=-1, keepdims=True)
    return centered / jnp.sqrt(variance + EPSILON)


def absorb(state, queries, keyval, allowed):
    running_top, running_total, accumulated = state
    head_count = queries.shape[1]
    head_size = queries.shape[2]
    row_count = keyval.shape[0]
    width_att = head_count * head_size
    key_rows = keyval[:, :width_att].reshape(row_count, head_count, head_size)
    val_rows = keyval[:, width_att:].reshape(row_count, head_count, head_size)
    scores = (
        jnp.einsum("qhd,khd->hqk", queries, key_rows, preferred_element_type=jnp.float32)
        * SCORE_SCALE
    )
    scores = jnp.where(allowed[None], scores, NEGATIVE)
    new_top = jnp.maximum(running_top, jnp.max(scores, axis=-1))
    factor = jnp.exp(running_top - new_top)
    weights = jnp.where(allowed[None], jnp.exp(scores - new_top[:, :, None]), 0.0)
    running_total = running_total * factor + jnp.sum(weights, axis=-1)
    weights_low = weights.astype(jnp.bfloat16)
    update = jnp.einsum("hqk,khd->qhd", weights_low, val_rows, preferred_element_type=jnp.float32)
    accumulated = accumulated * jnp.transpose(factor)[:, :, None] + update
    return (new_top, running_total, accumulated)


def per_device(
    suffix_x,
    suffix_query,
    suffix_keyval,
    prefix_keyval,
    prefix_hidden,
    kv_weight,
    out_weight,
    fc_weight,
    proj_weight,
    lengths,
    placement,
    owners,
    recompute,
):
    device_count = lax.axis_size("dev")
    my_device = lax.axis_index("dev")
    slots = suffix_x.shape[1]
    block_rows = prefix_keyval.shape[1]
    width_att = suffix_query.shape[2]
    head_count = width_att // HEAD_DIM
    device_ids = jnp.arange(device_count, dtype=jnp.int32)
    hits = placement[0][:, None] == device_ids[None, :]
    device_length = jnp.sum(jnp.where(hits, lengths[0][:, None], 0), axis=0)
    my_length = jnp.sum(jnp.where(device_ids == my_device, device_length, 0))
    block_ids = jnp.arange(owners.shape[1], dtype=jnp.int32)
    chosen = recompute[0]
    chosen_owner = jnp.sum(
        jnp.where(chosen[:, None] == block_ids[None, :], owners[0][None, :], 0), axis=1
    )
    stale_device = jnp.any(chosen_owner[:, None] == device_ids[None, :], axis=0)
    queries = suffix_query[0].reshape(slots, head_count, HEAD_DIM)
    normed_prefix = normalize(prefix_hidden[0]).astype(jnp.bfloat16)
    fresh = jnp.dot(normed_prefix, kv_weight, preferred_element_type=jnp.float32).astype(
        jnp.bfloat16
    )
    my_stale = jnp.any(chosen_owner == my_device)
    local_kv = jnp.where(my_stale, fresh, prefix_keyval[0])
    skip_device = jnp.zeros_like(stale_device)
    gathered = lax.all_gather(local_kv, "dev", axis=0, tiled=True)
    prefix_count = gathered.shape[0]
    row_device = jnp.arange(prefix_count, dtype=jnp.int32) // block_rows
    skipped = jnp.any((row_device[:, None] == device_ids[None, :]) & skip_device[None, :], axis=1)
    state = (
        jnp.full((head_count, slots), NEGATIVE, jnp.float32),
        jnp.zeros((head_count, slots), jnp.float32),
        jnp.zeros((slots, head_count, HEAD_DIM), jnp.float32),
    )
    key_block = 512 if prefix_count % 512 == 0 else prefix_count
    for block_start in range(0, prefix_count, key_block):
        kept = jnp.logical_not(skipped[block_start : block_start + key_block])
        allowed = jnp.broadcast_to(kept[None, :], (slots, key_block))
        state = absorb(state, queries, gathered[block_start : block_start + key_block], allowed)
    positions = jnp.arange(slots, dtype=jnp.int32)
    causal = (positions[None, :] <= positions[:, None]) & (positions[None, :] < my_length)
    state = absorb(state, queries, suffix_keyval[0], causal)
    final_top, final_total, accumulated = state
    attended = (
        (accumulated / jnp.transpose(final_total)[:, :, None])
        .reshape(slots, width_att)
        .astype(jnp.bfloat16)
    )
    projected = jnp.dot(attended, out_weight, preferred_element_type=jnp.float32)
    residual = suffix_x[0].astype(jnp.float32) + projected
    normed = normalize(residual).astype(jnp.bfloat16)
    fc_full, proj_full = (
        lax.all_gather(fc_weight, ("group", "dev"), axis=1, tiled=True),
        lax.all_gather(proj_weight, ("group", "dev"), axis=0, tiled=True),
    )
    inner = jnp.dot(normed, fc_full, preferred_element_type=jnp.float32)
    activated = jax.nn.gelu(inner, approximate=True).astype(jnp.bfloat16)
    feed_out = jnp.dot(activated, proj_full, preferred_element_type=jnp.float32)
    live = positions[:, None] < my_length
    return jnp.where(live, residual + feed_out, 0.0).astype(jnp.bfloat16)[None]


def solution(mesh):
    return jax.shard_map(
        per_device,
        mesh=mesh,
        in_specs=(
            P("group", "dev", None),
            P("group", "dev", None),
            P("group", "dev", None),
            P("group", "dev", None),
            P("group", "dev", None),
            P(),
            P(),
            P(None, ("group", "dev")),
            P(("group", "dev"), None),
            P("group", None),
            P("group", None),
            P("group", None),
            P("group", None),
        ),
        out_specs=P("group", "dev", None),
        check_vma=False,
    )
```

profile of v0, /device:TPU:0, one launch (start us, length us, event | category | flops | bytes accessed | tf_op | source)
XLA Modules:
  0.0 235.2 jit_solution(8602153443183435182)
XLA Ops:
  6.6 0.7 all-gather.3.cloned.1.call-update
  7.3 0.7 all-gather.5.cloned.1.call-update
  8.0 2.2 fusion.67
  10.3 2.0 copy.33
  12.3 2.1 copy.30
  14.6 0.6 compare_reduce_fusion
  15.6 4.5 %fusion.14 = bf16[8,2048]{1,0:T(8,128)(2,1)S(1)} fusion(bf16[1600,2048]{1,0:T(8,128)(2,1)} %param.18, bf16[1,8,2048]{2,1,0:T(8,128)(2,1)S(1)} %copy-done.5, pred[]{:T(512)} %compare_reduce_fusion, bf16[1,8,1600]{2,1,0:T(8,128)(2,1)S(1)} %copy-done.4, f32[8]{0:T(128)S(1)} %add_sqrt_fusion.1, f32[8]{0:T(128)S(1)} %broadcast_multiply_fusion.1), kind=kOutput, calls=%fused_computation.20 | convolution fusion | flops 52512768 | bytes 6644801 | tf_op jit(solution)/shard_map/dot_general | solution.py:76
  20.1 25.2 %all_gather.9 = bf16[128,2048]{1,0:T(8,128)(2,1)S(1)} all-gather(bf16[8,2048]{1,0:T(8,128)(2,1)S(1)} %fusion.14), channel_id=1, replica_groups=mesh['group'=2,'dev'=16] {'dev'}, dimensions={0}, use_global_device_ids=true | all-gather | bytes 557056 | tf_op jit(solution)/shard_map/all_gather | solution.py:82
  45.3 0.7 fusion.68
  46.1 1.8 copy.29
  47.9 2.0 copy.34
  49.9 0.8 copy.31
  50.8 0.6 fusion.56
  51.5 0.6 iota_compare_fusion.2
  52.2 1.6 bitcast_reduce_fusion
  53.9 2.0 fusion.8
  56.3 1.0 fusion.9
  57.3 1.1 fusion.26
  58.5 0.6 fusion.33
  59.6 1.1 fusion.69
  60.7 1.2 copy-done.1
  62.2 49.0 %all-gather.3.cloned.1.call-done = bf16[1600,3840]{0,1:T(8,128)(2,1)} async-done(((bf16[1600,120]{0,1:T(8,128)(2,1)}), bf16[1600,3840]{0,1:T(8,128)(2,1)}) %all-gather.3.cloned.1.call-update) | async-done | bytes 12288016 | tf_op jit(solution)/shard_map/all_gather | solution.py:109
  111.2 98.2 %all-gather.5.cloned.1.call-done = bf16[3840,1600]{1,0:T(8,128)(2,1)} async-done(((bf16[120,1600]{1,0:T(8,128)(2,1)}), bf16[3840,1600]{1,0:T(8,128)(2,1)}) %all-gather.5.cloned.1.call-update) | async-done | bytes 12288016 | tf_op jit(solution)/shard_map/all_gather | solution.py:110
  209.4 19.0 %fusion.13 = bf16[1,256,1600]{1,2,0:T(8,128)(2,1)} fusion(f32[256,1600]{0,1:T(8,128)} %copy-done.1, bf16[3840,1600]{1,0:T(8,128)(2,1)} %all-gather.5.cloned.1.call-done, bf16[1600,3840]{0,1:T(8,128)(2,1)} %all-gather.3.cloned.1.call-done, f32[256]{0:T(256)S(1)} %add_sqrt_fusion, f32[256]{0:T(256)S(1)} %broadcast_multiply_fusion, ...), kind=kOutput, calls=%fused_computation.18 | convolution fusion | flops 6302760960 | bytes 27035904 | tf_op jit(solution)/shard_map/dot_general | solution.py:114
  (36 shorter events, 2.0 us)
Async XLA Ops:
  6.5 52.6 %copy-start = (bf16[1024,1600]{0,1:T(8,128)(2,1)S(1)}, bf16[1024,1600]{0,1:T(8,128)(2,1)}, u32[]{:S(2)}) copy-start(bf16[1024,1600]{0,1:T(8,128)(2,1)} %param.19) | copy-start | bytes 9830404
  6.5 7.9 %copy-start.8 = (s32[1,2]{1,0:T(1,128)S(1)}, s32[1,2]{1,0:T(1,128)}, u32[]{:S(2)}) copy-start(s32[1,2]{1,0:T(1,128)} %param.25) | copy-start | bytes 28
  6.5 7.9 %copy-start.7 = (s32[1,16]{1,0:T(1,128)S(1)}, s32[1,16]{1,0:T(1,128)}, u32[]{:S(2)}) copy-start(s32[1,16]{1,0:T(1,128)} %param.24) | copy-start | bytes 196
  6.5 8.7 %copy-start.4 = (bf16[1,8,1600]{2,1,0:T(8,128)(2,1)S(1)}, bf16[1,8,1600]{2,1,0:T(8,128)(2,1)}, u32[]{:S(2)}) copy-start(bf16[1,8,1600]{2,1,0:T(8,128)(2,1)} %param.17) | copy-start | bytes 76804
  6.5 9.1 %copy-start.5 = (bf16[1,8,2048]{2,1,0:T(8,128)(2,1)S(1)}, bf16[1,8,2048]{2,1,0:T(8,128)(2,1)}, u32[]{:S(2)}) copy-start(bf16[1,8,2048]{2,1,0:T(8,128)(2,1)} %param.16) | copy-start | bytes 98308
  6.5 104.7 %all-gather.3.cloned.1.call-start = ((), (), s32[]{:S(2)}) async-start(), calls=%async_computation | async-start | bytes 13178880 | tf_op jit(solution)/shard_map/all_gather | solution.py:109
  7.3 202.1 %all-gather.5.cloned.1.call-start = ((), (), s32[]{:S(2)}) async-start(), calls=%async_computation.1 | async-start | bytes 13178880 | tf_op jit(solution)/shard_map/all_gather | solution.py:110
  15.6 35.2 %copy-start.9 = (s32[1,16]{1,0:T(1,128)S(1)}, s32[1,16]{1,0:T(1,128)}, u32[]{:S(2)}) copy-start(s32[1,16]{1,0:T(1,128)} %param.22) | copy-start | bytes 196
  15.6 35.1 %copy-start.10 = (s32[1,16]{1,0:T(1,128)S(1)}, s32[1,16]{1,0:T(1,128)}, u32[]{:S(2)}) copy-start(s32[1,16]{1,0:T(1,128)} %param.23) | copy-start | bytes 196
  55.9 1.4 copy-start.2
  57.3 1.1 copy-start.3
  58.5 1.2 copy-start.6
  60.7 1.2 copy-start.1
Sparse Core Ops, SparseCore 0:
  10.2 100.9 all-gather.2
  114.0 95.2 all-gather.4
where the time goes:
time: 236 us; the launch traced here: 235 us
  waiting for transfers between devices  149 us (63%)
  matrix products  29.9 us (13%)
  blocking collectives  25.2 us (11%)
  local copies, waits for them, and re-layouts  13.6 us (6%)
  between operations  13.6 us (6%)
  other arithmetic  4.28 us (2%)
    all_gather x1, waiting for transfers between devices, per_device(): lax.all_gather(proj_weight, ('group', 'dev'), axis=0, tiled=True)  98.2 us
    all_gather x1, waiting for transfers between devices, per_device(): lax.all_gather(fc_weight, ('group', 'dev'), axis=1, tiled=True)  49 us
    all_gather x1, blocking collectives, per_device(): gathered = lax.all_gather(local_kv, 'dev', axis=0, tiled=True)  25.2 us
    dot_general x1, matrix products, per_device(): feed_out = jnp.dot(activated, proj_full, preferred_element_type=jnp.float32)  19 us
    slice x3, local copies, waits for them, and re-layouts, absorb(): key_rows = keyval[:, :width_att].reshape(row_count, head_count, head_size)  6.07 us
  transfers between devices with their start and end apart: 2, of which 2 were waited for; matrix products, arithmetic and copies ran while one was open for 11% of the time, Pallas kernels for 0%

commit v1 on v0

--- a/solution.py
+++ b/solution.py
@@ -7,6 +7,28 @@
 NEGATIVE = -1e30
 EPSILON = 1e-05
 SCORE_SCALE = 0.125
+
+
+def in_order(pieces, dim):
+    shape = list(pieces.shape[1:])
+    shape[dim] *= pieces.shape[0]
+    return jnp.moveaxis(pieces, 0, dim).reshape(shape)
+
+
+def collected_by_bits(x, axis):
+    count = lax.axis_size(axis)
+    pieces = x[None]
+    for level in range(count.bit_length() - 1):
+        stride = 1 << level
+        theirs = lax.ppermute(pieces, axis, [(i, i ^ stride) for i in range(count)])
+        both = jnp.stack([pieces, theirs])
+        upper = lax.axis_index(axis) >> level & 1
+        pieces = jnp.where(upper == 0, both, both[::-1]).reshape(-1, *x.shape)
+    return pieces
+
+
+def gather_by_bits(x, axis, dim):
+    return in_order(collected_by_bits(x, axis), dim)
 
 
 def normalize(values_in):
@@ -107,7 +129,7 @@
     normed = normalize(residual).astype(jnp.bfloat16)
     fc_full, proj_full = (
         lax.all_gather(fc_weight, ("group", "dev"), axis=1, tiled=True),
-        lax.all_gather(proj_weight, ("group", "dev"), axis=0, tiled=True),
+        gather_by_bits(proj_weight, ("group", "dev"), 0),
     )
     inner = jnp.dot(normed, fc_full, preferred_element_type=jnp.float32)
     activated = jax.nn.gelu(inner, approximate=True).astype(jnp.bfloat16)

time: 236 us -> 449 us (1.90)
  waiting for transfers between devices: 149 us -> 327 us
  other arithmetic: 4.28 us -> 34.5 us
  starting transfers between devices: 0.08 us -> 11.1 us
    ppermute x0 -> x5, waiting for transfers between devices: none -> 326 us  [collected_by_bits(): theirs = lax.ppermute(pieces, axis, [(i, i ^ stride) for i in range(count)])]
    all_gather x1 -> x0, waiting for transfers between devices: 98.2 us -> none  [per_device(): lax.all_gather(proj_weight, ('group', 'dev'), axis=0, tiled=True)]
    all_gather x1, waiting for transfers between devices: 49 us -> 0.01 us  [per_device(): lax.all_gather(fc_weight, ('group', 'dev'), axis=1, tiled=True)]
    another operation x0 -> x6, other arithmetic: none -> 16.3 us  [collected_by_bits(): both = jnp.stack([pieces, theirs])]
    select_n x0 -> x4, other arithmetic: none -> 14 us  [collected_by_bits(): pieces = jnp.where(upper == 0, both, both[::-1]).reshape(-1, *x.shape)]
    ppermute x0 -> x5, starting transfers between devices: none -> 11.1 us  [collected_by_bits(): theirs = lax.ppermute(pieces, axis, [(i, i ^ stride) for i in range(count)])]
  transfers between devices with their start and end apart: 2 -> 6, of which waited for: 2 -> 5; matrix products, arithmetic and copies ran while one was open for 11% -> 13% of each run, Pallas kernels for 0% -> 0%
where the time goes in v1:
time: 449 us; the launch traced here: 448 us
  waiting for transfers between devices  327 us (73%)
  other arithmetic  34.5 us (8%)
  matrix products  30 us (7%)
  blocking collectives  21 us (5%)
  between operations  13.6 us (3%)
  local copies, waits for them, and re-layouts  11.2 us (2%)
  starting transfers between devices  11.1 us (2%)
    ppermute x5, waiting for transfers between devices, collected_by_bits(): theirs = lax.ppermute(pieces, axis, [(i, i ^ stride) for i in range(count)])  326 us
    all_gather x1, blocking collectives, per_device(): gathered = lax.all_gather(local_kv, 'dev', axis=0, tiled=True)  21 us
    dot_general x1, matrix products, per_device(): feed_out = jnp.dot(activated, proj_full, preferred_element_type=jnp.float32)  19 us
    another operation x6, other arithmetic, collected_by_bits(): both = jnp.stack([pieces, theirs])  16.3 us
    select_n x4, other arithmetic, collected_by_bits(): pieces = jnp.where(upper == 0, both, both[::-1]).reshape(-1, *x.shape)  14 us
    ppermute x5, starting transfers between devices, collected_by_bits(): theirs = lax.ppermute(pieces, axis, [(i, i ^ stride) for i in range(count)])  11.1 us
  transfers between devices with their start and end apart: 6, of which 5 were waited for; matrix products, arithmetic and copies ran while one was open for 13% of the time, Pallas kernels for 0%

profile of v1, /device:TPU:0, one launch (start us, length us, event | category | flops | bytes accessed | tf_op | source)
XLA Modules:
  0.0 448.3 jit_solution(13098763553106306503)
XLA Ops:
  7.8 1.7 collective-permute-done
  12.1 2.9 collective-permute-start.1
  15.0 21.2 %collective-permute-done.1 = bf16[2,120,1600]{2,1,0:T(8,128)(2,1)} collective-permute-done((bf16[2,120,1600]{2,1,0:T(8,128)(2,1)}, bf16[2,120,1600]{2,1,0:T(8,128)(2,1)}, u32[]{:S(2)}, u32[]{:S(2)}) %collective-permute-start.1) | collective-permute-done | bytes 768032 | tf_op jit(solution)/shard_map/ppermute | solution.py:23
  39.2 1.8 collective-permute-start.2
  41.0 69.7 %collective-permute-done.2 = bf16[4,120,1600]{2,1,0:T(8,128)(2,1)} collective-permute-done((bf16[4,120,1600]{2,1,0:T(8,128)(2,1)}, bf16[4,120,1600]{2,1,0:T(8,128)(2,1)}, u32[]{:S(2)}, u32[]{:S(2)}) %collective-permute-start.2) | collective-permute-done | bytes 1536032 | tf_op jit(solution)/shard_map/ppermute | solution.py:23
  110.7 2.2 pad_maximum_fusion.2
  112.9 2.3 reverse_select_fusion.2
  115.2 4.3 collective-permute-start.3
  119.5 144.0 %collective-permute-done.3 = bf16[8,120,1600]{2,1,0:T(8,128)(2,1)} collective-permute-done((bf16[8,120,1600]{2,1,0:T(8,128)(2,1)}, bf16[8,120,1600]{2,1,0:T(8,128)(2,1)}, u32[]{:S(2)}, u32[]{:S(2)}) %collective-permute-start.3) | collective-permute-done | bytes 3072032 | tf_op jit(solution)/shard_map/ppermute | solution.py:23
  263.5 3.6 pad_maximum_fusion.1
  267.1 3.9 reverse_select_fusion.1
  271.0 1.6 collective-permute-start.4
  273.6 2.0 copy.33
  275.6 2.1 copy.30
  278.9 4.5 %fusion.14 = bf16[8,2048]{1,0:T(8,128)(2,1)S(1)} fusion(bf16[1600,2048]{1,0:T(8,128)(2,1)} %param.18, bf16[1,8,2048]{2,1,0:T(8,128)(2,1)S(1)} %copy-done.7, pred[]{:T(512)} %compare_reduce_fusion, bf16[1,8,1600]{2,1,0:T(8,128)(2,1)S(1)} %copy-done.6, f32[8]{0:T(128)S(1)} %add_sqrt_fusion.1, f32[8]{0:T(128)S(1)} %broadcast_multiply_fusion.1), kind=kOutput, calls=%fused_computation.27 | convolution fusion | flops 52512768 | bytes 6644801 | tf_op jit(solution)/shard_map/dot_general | solution.py:98
  283.5 21.0 %all_gather.6 = bf16[128,2048]{1,0:T(8,128)(2,1)S(1)} all-gather(bf16[8,2048]{1,0:T(8,128)(2,1)S(1)} %fusion.14), channel_id=1, replica_groups=mesh['group'=2,'dev'=16] {'dev'}, dimensions={0}, use_global_device_ids=true | all-gather | bytes 557056 | tf_op jit(solution)/shard_map/all_gather | solution.py:104
  305.2 1.8 copy.29
  307.0 2.0 copy.34
  311.4 1.6 bitcast_reduce_fusion
  313.0 2.0 fusion.8
  320.1 89.6 %collective-permute-done.4 = bf16[16,120,1600]{2,1,0:T(8,128)(2,1)} collective-permute-done((bf16[16,120,1600]{2,1,0:T(8,128)(2,1)}, bf16[16,120,1600]{2,1,0:T(8,128)(2,1)}, u32[]{:S(2)}, u32[]{:S(2)}) %collective-permute-start.4) | collective-permute-done | bytes 6144032 | tf_op jit(solution)/shard_map/ppermute | solution.py:23
  409.7 6.3 %pad_maximum_fusion = bf16[2,16,120,1600]{3,2,1,0:T(8,128)(2,1)S(1)} fusion(bf16[1,16,120,1600]{3,2,1,0:T(8,128)(2,1)} %bitcast.35, bf16[1,16,120,1600]{3,2,1,0:T(8,128)(2,1)} %bitcast.33), kind=kLoop, calls=%fused_computation.1 | loop fusion | flops 6144000 | bytes 24576000 | tf_op jit(solution)/shard_map/stack | solution.py:24
  416.1 6.3 %reverse_select_fusion = bf16[2,16,120,1600]{3,2,1,0:T(8,128)(2,1)} fusion(bf16[2,16,120,1600]{3,2,1,0:T(8,128)(2,1)S(1)} %pad_maximum_fusion, pred[]{:T(512)S(6)} %eq.69), kind=kLoop, calls=%fused_computation | loop fusion | flops 6144000 | bytes 24576000 | tf_op jit(solution)/shard_map/jit(_where)/select_n | solution.py:26
  422.4 19.0 %fusion.13 = bf16[1,256,1600]{1,2,0:T(8,128)(2,1)} fusion(f32[256,1600]{0,1:T(8,128)} %copy-done.2, bf16[3840,1600]{1,0:T(8,128)(2,1)} %bitcast.105, bf16[1600,3840]{0,1:T(8,128)(2,1)} %all-gather.2.cloned.1.call-done, f32[256]{0:T(256)S(1)} %add_sqrt_fusion, f32[256]{0:T(256)S(1)} %broadcast_multiply_fusion, pred[256]{0:T(512)(128)(4,1)S(1)} %iota_compare_fusion.2), kind=kOutput, calls=%fused_computation.24 | convolution fusion | flops 6302760960 | bytes 27035904 | tf_op jit(solution)/shard_map/dot_general | solution.py:136
  (57 shorter events, 17.1 us)
Async XLA Ops:
  6.5 311.7 %copy-start = (bf16[1024,1600]{0,1:T(8,128)(2,1)S(1)}, bf16[1024,1600]{0,1:T(8,128)(2,1)}, u32[]{:S(2)}) copy-start(bf16[1024,1600]{0,1:T(8,128)(2,1)} %param.19) | copy-start | bytes 9830404
  6.5 415.9 %all-gather.2.cloned.1.call-start = ((), (), s32[]{:S(2)}) async-start(), calls=%async_computation | async-start | bytes 13178880 | tf_op jit(solution)/shard_map/all_gather | solution.py:131
  7.3 2.2 collective-permute-start
  12.1 24.2 %collective-permute-start.1 = (bf16[2,120,1600]{2,1,0:T(8,128)(2,1)}, bf16[2,120,1600]{2,1,0:T(8,128)(2,1)}, u32[]{:S(2)}, u32[]{:S(2)}) collective-permute-start(bf16[2,120,1600]{2,1,0:T(8,128)(2,1)} %get-tuple-element.10), channel_id=1, source_target_pairs={{0,2},{1,3},{2,0},{3,1},{4,6},{5,7},{6,4},{7,5},{8,10},{9,11},{10,... | collective-permute-start | bytes 2304008 | tf_op jit(solution)/shard_map/ppermute | solution.py:23
  39.2 71.5 %collective-permute-start.2 = (bf16[4,120,1600]{2,1,0:T(8,128)(2,1)}, bf16[4,120,1600]{2,1,0:T(8,128)(2,1)}, u32[]{:S(2)}, u32[]{:S(2)}) collective-permute-start(bf16[4,120,1600]{2,1,0:T(8,128)(2,1)} %bitcast.28), channel_id=1, source_target_pairs={{0,4},{1,5},{2,6},{3,7},{4,0},{5,1},{6,2},{7,3},{8,12},{9,13},{10,... | collective-permute-start | bytes 4608008 | tf_op jit(solution)/shard_map/ppermute | solution.py:23
  115.2 148.3 %collective-permute-start.3 = (bf16[8,120,1600]{2,1,0:T(8,128)(2,1)}, bf16[8,120,1600]{2,1,0:T(8,128)(2,1)}, u32[]{:S(2)}, u32[]{:S(2)}) collective-permute-start(bf16[8,120,1600]{2,1,0:T(8,128)(2,1)} %bitcast.31), channel_id=1, source_target_pairs={{0,8},{1,9},{2,10},{3,11},{4,12},{5,13},{6,14},{7,15},{8,0},{9,1},... | collective-permute-start | bytes 9216008 | tf_op jit(solution)/shard_map/ppermute | solution.py:23
  267.1 5.5 %copy-start.3 = (bf16[1,256,2048]{2,1,0:T(8,128)(2,1)S(1)}, bf16[1,256,2048]{2,1,0:T(8,128)(2,1)}, u32[]{:S(2)}) copy-start(bf16[1,256,2048]{2,1,0:T(8,128)(2,1)} %param.15) | copy-start | bytes 3145732
  271.0 6.8 %copy-start.9 = (s32[1,16]{1,0:T(1,128)S(1)}, s32[1,16]{1,0:T(1,128)}, u32[]{:S(2)}) copy-start(s32[1,16]{1,0:T(1,128)} %param.24) | copy-start | bytes 196
  271.0 6.8 %copy-start.10 = (s32[1,2]{1,0:T(1,128)S(1)}, s32[1,2]{1,0:T(1,128)}, u32[]{:S(2)}) copy-start(s32[1,2]{1,0:T(1,128)} %param.25) | copy-start | bytes 28
  271.0 7.6 %copy-start.6 = (bf16[1,8,1600]{2,1,0:T(8,128)(2,1)S(1)}, bf16[1,8,1600]{2,1,0:T(8,128)(2,1)}, u32[]{:S(2)}) copy-start(bf16[1,8,1600]{2,1,0:T(8,128)(2,1)} %param.17) | copy-start | bytes 76804
  271.0 7.9 %copy-start.7 = (bf16[1,8,2048]{2,1,0:T(8,128)(2,1)S(1)}, bf16[1,8,2048]{2,1,0:T(8,128)(2,1)}, u32[]{:S(2)}) copy-start(bf16[1,8,2048]{2,1,0:T(8,128)(2,1)} %param.16) | copy-start | bytes 98308
  271.0 138.8 %collective-permute-start.4 = (bf16[16,120,1600]{2,1,0:T(8,128)(2,1)}, bf16[16,120,1600]{2,1,0:T(8,128)(2,1)}, u32[]{:S(2)}, u32[]{:S(2)}) collective-permute-start(bf16[16,120,1600]{2,1,0:T(8,128)(2,1)} %bitcast.34), channel_id=1, source_target_pairs={{0,16},{1,17},{2,18},{3,19},{4,20},{5,21},{6,22},{7,23},{8,24},{9,... | collective-permute-start | bytes 18432008 | tf_op jit(solution)/shard_map/ppermute | solution.py:23
  278.9 31.0 %copy-start.11 = (s32[1,16]{1,0:T(1,128)S(1)}, s32[1,16]{1,0:T(1,128)}, u32[]{:S(2)}) copy-start(s32[1,16]{1,0:T(1,128)} %param.22) | copy-start | bytes 196
  278.9 31.0 %copy-start.12 = (s32[1,16]{1,0:T(1,128)S(1)}, s32[1,16]{1,0:T(1,128)}, u32[]{:S(2)}) copy-start(s32[1,16]{1,0:T(1,128)} %param.23) | copy-start | bytes 196
  315.1 1.4 copy-start.4
  316.5 1.1 copy-start.5
  317.6 1.2 copy-start.8
  319.9 89.9 %copy-start.2 = (f32[256,1600]{0,1:T(8,128)}, f32[256,1600]{0,1:T(8,128)S(1)}, u32[]{:S(2)}) copy-start(f32[256,1600]{0,1:T(8,128)S(1)} %get-tuple-element.21) | copy-start | bytes 4915204
  422.4 19.0 %copy-start.1 = (bf16[1024,1600]{0,1:T(8,128)(2,1)S(1)}, bf16[1024,1600]{0,1:T(8,128)(2,1)}, u32[]{:S(2)}) copy-start(bf16[1024,1600]{0,1:T(8,128)(2,1)} %param.19) | copy-start | bytes 9830404
Sparse Core Ops, SparseCore 0:
  10.2 192.7 all-gather.1
